TPU v7x, 32 devices: a whole 2x2x4 slice. The times are simulated.
32 devices in a mesh: freq: 2 (over y), gx: 4 (over z), gy: 2 (over x), col: 2 (over core).
Axes of the slice: x: 2, y: 2, z: 4, core: 2. Of those that a mesh axis runs over, the one named last changes fastest.
Arguments:
- source: bfloat16 [12, 64, 32, 256], P('freq', 'gx', 'gy', 'col'), parts along dimension 0, may hold values from -6 to 6
- warm: bfloat16 [12, 64, 32, 256], P('freq', 'gx', 'gy', 'col'), parts along dimension 0, may hold values from -2.1 to 2.6
- forward: bfloat16 [12, 64, 32, 256], P('freq', 'gx', 'gy', 'col'), parts along dimension 0, may hold values from -6 to 6
- density: bfloat16 [64, 32, 256], P('gx', 'gy', 'col'), may hold values from 1 to 3
- material_map: int32 [8, 4, 8], P('gx', 'gy', 'col'), may hold values from 0 to 7
- material_table: float32 [8, 2], replicated, may hold values from 0.5 to 2
- iface_cells: int32 [16, 256], P(('gx', 'gy', 'col')), may hold values from 0 to 32767, as said below
- impedance: float32 [2, 3], replicated, may hold values from 2 to 8
- omega2: float32 [2], P('freq'), parts along dimension 0, may hold values from 0.5 to 1
Outputs:
- adjoint: float32 [12, 64, 32, 256], P('freq', 'gx', 'gy', 'col'), parts along dimension 0
- coarse_gradient: float32 [32, 8], P('freq'), parts along dimension 0
There are 2 independent parts, one for each index of `freq`. A program takes and returns all parts, laid end to end along the dimension named above; an argument that names none is the same for every part. Nothing has to cross between parts.
Inputs may be any that keep to these rules, and one draw needn't show every extreme that they name: `iface_cells`: each row's entries are distinct, rising, and within the tile of 16 x 16 x 128 cells; row r belongs to the device of that index along gx, gy and col together.
All inputs are finite; a program needn't handle non-finite values.
Results may differ from a plain program's by a relative error of at most 0.0003.
Values may be sent and summed in bfloat16 or wider, within the bound.
No kernel may reach another device: no remote copies, remote signals or barrier semaphores. Data moves between devices by JAX's collectives and lax.ppermute only.
A program may use at most 64 MiB of HBM per device.

v0:
```python
import jax
import jax.numpy as jnp
from jax import lax
from jax.sharding import PartitionSpec as P

DAMPING = 0.5
RELAXATION = 0.6


def with_halo(array, sides, width):
    for axis, dim in sides:
        peers, length = (lax.axis_size(axis), array.shape[dim])
        up = [(i, (i + 1) % peers) for i in range(peers - 1)]
        down = [(j, i) for i, j in up]
        last = lax.slice_in_dim(array, length - width, length, axis=dim)
        initial = lax.slice_in_dim(array, 0, width, axis=dim)
        before = lax.ppermute(last, axis, up)
        after = lax.ppermute(initial, axis, down)
        array = jnp.concatenate([before, array, after], axis=dim)
    return array


def window(padded, offset):
    size_x = padded.shape[1] - 2
    size_y = padded.shape[2] - 2
    size_z = padded.shape[3] - 2
    return padded[
        :,
        1 + offset[0] : 1 + offset[0] + size_x,
        1 + offset[1] : 1 + offset[1] + size_y,
        1 + offset[2] : 1 + offset[2] + size_z,
    ]


def navier(padded, lame_first, shear):
    units = ((1, 0, 0), (0, 1, 0), (0, 0, 1))
    centre = window(padded, (0, 0, 0))
    second = []
    for axis_d in range(3):
        ahead = units[axis_d]
        behind = tuple((-value for value in ahead))
        second.append(window(padded, ahead) + window(padded, behind) - 2.0 * centre)
    laplace = second[0] + second[1] + second[2]
    result = []
    for part_index in range(2):
        for component in range(3):
            channel = part_index * 3 + component
            divergence = second[component][channel]
            for other_axis in range(3):
                if other_axis != component:
                    source_channel = part_index * 3 + other_axis
                    single = padded[source_channel : source_channel + 1]
                    first_unit = units[component]
                    other_unit = units[other_axis]
                    plus_plus = tuple((first_unit[k] + other_unit[k] for k in range(3)))
                    plus_minus = tuple((first_unit[k] - other_unit[k] for k in range(3)))
                    minus_plus = tuple((-first_unit[k] + other_unit[k] for k in range(3)))
                    minus_minus = tuple((-first_unit[k] - other_unit[k] for k in range(3)))
                    mixed = (
                        window(single, plus_plus)
                        - window(single, plus_minus)
                        - window(single, minus_plus)
                        + window(single, minus_minus)
                    )
                    divergence = divergence + 0.25 * mixed[0]
            result.append(shear * laplace[channel] + (lame_first + shear) * divergence)
    return jnp.stack(result)


def sweep(padded, lame_first, shear, density, mask, source, mean_field, omega_sq, impedance):
    field = window(padded, (0, 0, 0))
    elastic = navier(padded, lame_first, shear)
    real_part = field[:3]
    imag_part = field[3:]
    mean_real = mean_field[:3][:, None, None, None]
    mean_imag = mean_field[3:][:, None, None, None]
    imp_real = impedance[0][:, None, None, None]
    imp_imag = impedance[1][:, None, None, None]
    inertia = omega_sq * density
    diff_real = real_part - mean_real
    diff_imag = imag_part - mean_imag
    apply_real = (
        -elastic[:3]
        - inertia * (real_part - DAMPING * imag_part)
        + mask * (imp_real * diff_real - imp_imag * diff_imag)
    )
    apply_imag = (
        -elastic[3:]
        - inertia * (imag_part + DAMPING * real_part)
        + mask * (imp_real * diff_imag + imp_imag * diff_real)
    )
    resid_real = source[:3] - apply_real
    resid_imag = source[3:] - apply_imag
    diag_real = 8.0 * shear + 2.0 * lame_first - inertia + mask * imp_real
    diag_imag = -DAMPING * inertia + mask * imp_imag
    modulus = diag_real * diag_real + diag_imag * diag_imag
    new_real = real_part + RELAXATION * (resid_real * diag_real + resid_imag * diag_imag) / modulus
    new_imag = imag_part + RELAXATION * (resid_imag * diag_real - resid_real * diag_imag) / modulus
    return jnp.concatenate([new_real, new_imag], 0)


def expand(blocks):
    blocks_x, blocks_y, blocks_z = blocks.shape
    spread = jnp.broadcast_to(
        blocks[:, None, :, None, :, None], (blocks_x, 8, blocks_y, 8, blocks_z, 32)
    )
    return spread.reshape(blocks_x * 8, blocks_y * 8, blocks_z * 32)


def material(block_ids, table):
    lame_first = jnp.zeros(block_ids.shape, jnp.float32)
    shear = jnp.zeros(block_ids.shape, jnp.float32)
    for entry in range(table.shape[0]):
        chosen = block_ids == entry
        lame_first = jnp.where(chosen, table[entry, 0], lame_first)
        shear = jnp.where(chosen, table[entry, 1], shear)
    return (lame_first, shear)


def foundation(field, mask, count):
    total = lax.psum(jnp.sum(mask * field, axis=(1, 2, 3)), ("gx", "gy", "col"))
    return total / count


def shards(
    source, warm, forward, density, material_map, material_table, iface_cells, impedance, omega2
):
    omega_sq = omega2[0]
    tile_shape = density.shape
    tile_cells = tile_shape[0] * tile_shape[1] * tile_shape[2]
    mask = jnp.zeros((tile_cells,), jnp.float32).at[iface_cells[0]].set(1.0).reshape(tile_shape)
    block_ids = expand(material_map)
    lame_first, shear = material(block_ids, material_table)
    density_cells = density.astype(jnp.float32)
    source_cells = source.astype(jnp.float32)
    group_size = lax.axis_size("gx") * lax.axis_size("gy") * lax.axis_size("col")
    count = jnp.float32(group_size * iface_cells.shape[1])
    field = warm.astype(jnp.float32)
    for sweep_index in range(2):
        mean_field = foundation(field, mask, count)
        padded = with_halo(field, (("gx", 1), ("gy", 2), ("col", 3)), 1)
        field = sweep(
            padded,
            lame_first,
            shear,
            density_cells,
            mask,
            source_cells,
            mean_field,
            omega_sq,
            impedance,
        )
    forward_cells = forward.astype(jnp.float32)
    correlation = (
        field[:3] * forward_cells[:3]
        - field[3:] * forward_cells[3:]
        - DAMPING * (field[:3] * forward_cells[3:] + field[3:] * forward_cells[:3])
    )
    cell_terms = -omega_sq * jnp.sum(correlation, axis=0)
    coarse_x = tile_shape[0] // 4
    coarse_y = tile_shape[1] // 4
    local_sums = cell_terms.reshape(coarse_x, 4, coarse_y, 4, tile_shape[2]).sum(axis=(1, 3, 4))
    paired = lax.psum(local_sums, "col")
    gathered = lax.all_gather(paired[None], ("gx", "gy"), axis=0, tiled=True)
    grid_sums = gathered.reshape(lax.axis_size("gx"), lax.axis_size("gy"), coarse_x, coarse_y)
    coarse = (
        grid_sums.transpose(0, 2, 1, 3).reshape(
            lax.axis_size("gx") * coarse_x, lax.axis_size("gy") * coarse_y
        )
        / 64.0
    )
    return (field, coarse)


def solution(mesh):
    in_specs = (
        P("freq", "gx", "gy", "col"),
        P("freq", "gx", "gy", "col"),
        P("freq", "gx", "gy", "col"),
        P("gx", "gy", "col"),
        P("gx", "gy", "col"),
        P(),
        P(("gx", "gy", "col"), None),
        P(),
        P("freq"),
    )
    out_specs = (P("freq", "gx", "gy", "col"), P("freq", None))
    return jax.shard_map(shards, mesh=mesh, in_specs=in_specs, out_specs=out_specs, check_vma=False)
```

profile of v0, /device:TPU:0, one launch (start us, length us, event | category | flops | bytes accessed | tf_op | source)
XLA Modules:
  0.0 208.3 jit_solution(2462226845284078183)
XLA Ops:
  2.7 5.6 %collective-permute-start.1 = (f32[6,1,16,128]{3,2,1,0:T(8,128)S(1)}, f32[6,1,16,128]{3,2,1,0:T(8,128)S(1)}, u32[]{:S(2)}, u32[]{:S(2)}) collective-permute-start(f32[6,1,16,128]{3,2,1,0:T(8,128)S(1)} %get-tuple-element.40), channel_id=1, source_target_pairs={{0,4},{4,8},{8,12},{1,5},{5,9},{9,13},{2,6},{6,10},{10,14},{3,7},{... | collective-permute-start | bytes 147464 | tf_op jit(solution)/shard_map/ppermute | solution.py:17
  8.3 2.0 fusion.108
  11.0 1.9 broadcast_select_fusion
  12.9 4.6 %select_select_fusion.1 = f32[2,8,2,8,4,32]{5,4,3,2,1,0:T(4,128)S(1)} fusion(f32[]{:T(128)} %bitcast, f32[]{:T(128)} %bitcast.1, f32[]{:T(128)} %bitcast.2, f32[]{:T(128)} %bitcast.3, f32[]{:T(128)} %bitcast.4, f32[2,2,4]{2,1,0:T(2,128)S(1)} %get-tuple-element.46, f32[]{:T(128)} %bitcast.6, f32[]{:T(128)} %bitcast.5, ...), kind=kLoop, calls=%fused_computation.41 | loop fusion | flops 229376 | bytes 131276 | tf_op jit(solution)/shard_map/jit(_where)/select_n | solution.py:116
  17.4 4.5 %select_select_fusion = f32[2,8,2,8,4,32]{5,4,3,2,1,0:T(4,128)S(1)} fusion(f32[]{:T(128)} %bitcast.8, f32[]{:T(128)} %bitcast.9, f32[]{:T(128)} %bitcast.10, f32[]{:T(128)} %bitcast.11, f32[]{:T(128)} %bitcast.12, f32[2,2,4]{2,1,0:T(2,128)S(1)} %get-tuple-element.45, f32[]{:T(128)} %bitcast.14, f32[]{:T(128)} %bitcast.13, ...), kind=kLoop, calls=%fused_computation.40 | loop fusion | flops 229376 | bytes 131276 | tf_op jit(solution)/shard_map/jit(_where)/select_n | solution.py:115
  22.0 8.9 %multiply_add_fusion = f32[2,8,2,8,4,32]{5,4,3,2,1,0:T(4,128)S(1)} fusion(f32[2,2,4]{2,1,0:T(2,128)S(1)} %get-tuple-element.46, f32[]{:T(128)} %bitcast.6, pred[2,2,4]{2,1,0:T(4,128)(4,1)S(1)} %get-tuple-element.53, f32[]{:T(128)} %bitcast.5, pred[2,2,4]{2,1,0:T(4,128)(4,1)S(1)} %get-tuple-element.48, f32[]{:T(128)} %bitcast.4, ...), kind=kLoop, calls=%fused_computation.39 | loop fusion | flops 557056 | bytes 131368 | tf_op jit(solution)/shard_map/add | solution.py:94
  34.1 5.8 %collective-permute-start.3 = (f32[6,18,1,128]{3,2,1,0:T(1,128)S(1)}, f32[6,18,1,128]{3,2,1,0:T(1,128)}, u32[]{:S(2)}, u32[]{:S(2)}) collective-permute-start(f32[6,18,1,128]{3,2,1,0:T(1,128)S(1)} %get-tuple-element.34), channel_id=1, source_target_pairs={{0,2},{1,3},{4,6},{5,7},{8,10},{9,11},{12,14},{13,15},{16,18},{17,... | collective-permute-start | bytes 165896 | tf_op jit(solution)/shard_map/ppermute | solution.py:17
  42.7 2.0 scatter_custom_fusion
  50.0 3.6 %collective-permute-start.5 = (f32[6,18,18,1]{2,1,3,0:T(8,128)S(1)}, f32[6,18,18,1]{2,1,3,0:T(8,128)}, u32[]{:S(2)}, u32[]{:S(2)}) collective-permute-start(f32[6,18,18,1]{2,1,3,0:T(8,128)S(1)} %copy.46), channel_id=1, source_target_pairs={{0,1},{2,3},{4,5},{6,7},{8,9},{10,11},{12,13},{14,15},{16,17},{18,... | collective-permute-start | bytes 23336 | tf_op jit(solution)/shard_map/ppermute | solution.py:17
  53.7 2.6 %pad_maximum_fusion.2 = (f32[6,18,17,128]{3,2,1,0:T(8,128)}, f32[6,18,17,128]{3,2,1,0:T(8,128)}) fusion(f32[6,18,1,128]{3,2,1,0:T(1,128)} %collective-permute-done.2, f32[6,1,16,128]{3,2,1,0:T(8,128)S(1)} %collective-permute-done, f32[6,16,16,128]{3,2,1,0:T(8,128)S(1)} %convert_element_type.12, f32[6,1,16,128]{3,2,1,0:T(8,128)S(1)} %collective-permute-done.1, ...), kind=kLoop, calls=%fused_computation.5 | loop fusion | flops 1410048 | bytes 2875392 | tf_op jit(solution)/shard_map/concatenate | solution.py:19
  58.7 3.1 %pad_maximum_fusion = (f32[6,18,18,129]{3,2,1,0:T(8,128)S(1)}, f32[6,18,18,129]{3,2,1,0:T(8,128)S(1)}) fusion(f32[6,18,18,1]{3,2,1,0:T(8,128)S(1)} %copy.45, f32[6,18,1,128]{3,2,1,0:T(1,128)} %collective-permute-done.2, f32[6,1,16,128]{3,2,1,0:T(8,128)S(1)} %collective-permute-done, f32[6,16,16,128]{3,2,1,0:T(8,128)S(1)} %convert_element_type.12, ...), kind=kLoop, calls=%fused_computation.1 | loop fusion | flops 2507760 | bytes 3017088 | tf_op jit(solution)/shard_map/concatenate | solution.py:19
  61.8 2.3 %add_add_fusion.1 = (f32[6,16,16,128]{3,2,1,0:T(8,128)}, f32[6,16,16,128]{3,2,1,0:T(8,128)}, f32[6,16,16,128]{3,2,1,0:T(8,128)}, f32[6,16,16,128]{3,2,1,0:T(8,128)}, f32[6]{0:T(128)S(1)}) fusion(bf16[6,16,16,128]{3,2,1,0:T(8,128)(2,1)S(1)} %copy-done.28, f32[6,18,17,128]{3,2,1,0:T(8,128)S(1)} %copy-done.17, f32[6,18,17,128]{3,2,1,0:T(8,128)S(1)} %copy-done.16, ...), kind=kLoop, calls=%fused_computation.38 | loop fusion | flops 2949114 | bytes 7700504 | tf_op jit(solution)/shard_map/add | solution.py:43
  64.2 29.5 %psum.21 = f32[6]{0:T(128)S(1)} all-reduce(f32[6]{0:T(128)S(1)} %get-tuple-element.39), channel_id=1, replica_groups=mesh['freq'=2,'gx'=4,'gy'=2,'col'=2] {'gx','gy','col'}, use_global_device_ids=true, to_apply=%region_2.3 | all-reduce | flops 6 | bytes 48 | tf_op jit(solution)/shard_map/psum | solution.py:121
  99.7 1.7 fusion.77
  101.5 1.7 fusion.59
  105.5 4.5 %collective-permute-start.7 = (f32[6,1,16,128]{3,2,1,0:T(8,128)S(1)}, f32[6,1,16,128]{3,2,1,0:T(8,128)S(1)}, u32[]{:S(2)}, u32[]{:S(2)}) collective-permute-start(f32[6,1,16,128]{3,2,1,0:T(8,128)S(1)} %get-tuple-element.37), channel_id=1, source_target_pairs={{0,4},{4,8},{8,12},{1,5},{5,9},{9,13},{2,6},{6,10},{10,14},{3,7},{... | collective-permute-start | bytes 147464 | tf_op jit(solution)/shard_map/ppermute | solution.py:17
  113.2 4.7 %collective-permute-start.9 = (f32[6,18,1,128]{3,2,1,0:T(1,128)S(1)}, f32[6,18,1,128]{3,2,1,0:T(1,128)S(1)}, u32[]{:S(2)}, u32[]{:S(2)}) collective-permute-start(f32[6,18,1,128]{3,2,1,0:T(1,128)S(1)} %get-tuple-element.30), channel_id=1, source_target_pairs={{0,2},{1,3},{4,6},{5,7},{8,10},{9,11},{12,14},{13,15},{16,18},{17,... | collective-permute-start | bytes 165896 | tf_op jit(solution)/shard_map/ppermute | solution.py:17
  124.8 3.6 %collective-permute-start.11 = (f32[6,18,18,1]{2,1,3,0:T(8,128)S(1)}, f32[6,18,18,1]{2,1,3,0:T(8,128)}, u32[]{:S(2)}, u32[]{:S(2)}) collective-permute-start(f32[6,18,18,1]{2,1,3,0:T(8,128)S(1)} %copy.50), channel_id=1, source_target_pairs={{0,1},{2,3},{4,5},{6,7},{8,9},{10,11},{12,13},{14,15},{16,17},{18,... | collective-permute-start | bytes 23336 | tf_op jit(solution)/shard_map/ppermute | solution.py:17
  128.4 1.7 pad_maximum_fusion.4
  132.6 3.6 %pad_maximum_fusion.1 = (f32[6,18,18,129]{3,2,1,0:T(8,128)S(1)}, f32[6,18,18,129]{3,2,1,0:T(8,128)S(1)}) fusion(f32[6,18,18,1]{3,2,1,0:T(8,128)S(1)} %copy.49, f32[6,18,1,128]{3,2,1,0:T(1,128)} %copy-done.10, f32[6,1,16,128]{3,2,1,0:T(8,128)S(1)} %collective-permute-done.6, f32[3,16,16,128]{3,2,1,0:T(8,128)S(1)} %divide_add_fusion.2, ...), kind=kLoop, calls=%fused_computation.3 | loop fusion | flops 3009312 | bytes 3017088 | tf_op jit(solution)/shard_map/concatenate | solution.py:19
  136.3 2.3 %add_add_fusion = (f32[6,16,16,128]{3,2,1,0:T(8,128)}, f32[6,16,16,128]{3,2,1,0:T(8,128)}, f32[6,16,16,128]{3,2,1,0:T(8,128)}, f32[6,16,16,128]{3,2,1,0:T(8,128)}, f32[6]{0:T(128)S(1)}) fusion(f32[3,16,16,128]{3,2,1,0:T(8,128)S(1)} %divide_add_fusion.2, f32[3,16,16,128]{3,2,1,0:T(8,128)S(1)} %get-tuple-element.11, f32[6,18,17,128]{3,2,1,0:T(8,128)S(1)} %copy-done.19, ...), kind=kLoop, calls=%fused_computation.36 | loop fusion | flops 3145722 | bytes 7307288 | tf_op jit(solution)/shard_map/add | solution.py:43
  138.6 29.5 %psum.22 = f32[6]{0:T(128)S(1)} all-reduce(f32[6]{0:T(128)S(1)} %get-tuple-element.36), channel_id=1, replica_groups=mesh['freq'=2,'gx'=4,'gy'=2,'col'=2] {'gx','gy','col'}, use_global_device_ids=true, to_apply=%region_4.5 | all-reduce | flops 6 | bytes 48 | tf_op jit(solution)/shard_map/psum | solution.py:121
  178.1 2.4 %psum.23 = f32[1,4,4]{2,1,0:T(4,128)S(1)} all-reduce(f32[1,4,4]{2,1,0:T(4,128)S(1)} %bitcast.39), channel_id=1, replica_groups=mesh['freq'=2,'gx'=4,'gy'=2,'col'=2] {'col'}, use_global_device_ids=true, to_apply=%region_8.9 | all-reduce | flops 16 | bytes 128 | tf_op jit(solution)/shard_map/psum | solution.py:163
  180.5 26.0 %all_gather.3 = f32[8,4,4]{2,1,0:T(4,128)S(1)} all-gather(f32[1,4,4]{2,1,0:T(4,128)S(1)} %psum.23), channel_id=1, replica_groups=mesh['freq'=2,'gx'=4,'gy'=2,'col'=2] {'gx','gy'}, dimensions={0}, use_global_device_ids=true | all-gather | bytes 576 | tf_op jit(solution)/shard_map/all_gather | solution.py:164
  (141 shorter events, 48.0 us)
Async XLA Ops:
  0.6 31.2 %copy-start.33 = (bf16[16,16,128]{2,1,0:T(8,128)(2,1)S(1)}, bf16[16,16,128]{2,1,0:T(8,128)(2,1)}, u32[]{:S(2)}) copy-start(bf16[16,16,128]{2,1,0:T(8,128)(2,1)} %param.12) | copy-start | bytes 196612
  1.4 31.2 %collective-permute-start = (f32[6,1,16,128]{3,2,1,0:T(8,128)S(1)}, f32[6,1,16,128]{3,2,1,0:T(8,128)S(1)}, u32[]{:S(2)}, u32[]{:S(2)}) collective-permute-start(f32[6,1,16,128]{3,2,1,0:T(8,128)S(1)} %get-tuple-element.41), channel_id=1, source_target_pairs={{4,0},{8,4},{12,8},{5,1},{9,5},{13,9},{6,2},{10,6},{14,10},{7,3},{... | collective-permute-start | bytes 147464 | tf_op jit(solution)/shard_map/ppermute | solution.py:18
  2.7 30.0 %collective-permute-start.1 = (f32[6,1,16,128]{3,2,1,0:T(8,128)S(1)}, f32[6,1,16,128]{3,2,1,0:T(8,128)S(1)}, u32[]{:S(2)}, u32[]{:S(2)}) collective-permute-start(f32[6,1,16,128]{3,2,1,0:T(8,128)S(1)} %get-tuple-element.40), channel_id=1, source_target_pairs={{0,4},{4,8},{8,12},{1,5},{5,9},{9,13},{2,6},{6,10},{10,14},{3,7},{... | collective-permute-start | bytes 147464 | tf_op jit(solution)/shard_map/ppermute | solution.py:17
  12.9 19.7 %copy-start.34 = (s32[1,256]{1,0:T(1,128)S(1)}, s32[1,256]{1,0:T(1,128)}, u32[]{:S(2)}) copy-start(s32[1,256]{1,0:T(1,128)} %param.15) | copy-start | bytes 3076
  12.9 19.7 %copy-start.27 = (bf16[6,16,16,128]{3,2,1,0:T(8,128)(2,1)S(1)}, bf16[6,16,16,128]{3,2,1,0:T(8,128)(2,1)}, u32[]{:S(2)}) copy-start(bf16[6,16,16,128]{3,2,1,0:T(8,128)(2,1)} %param.10) | copy-start | bytes 1179652
  31.8 8.1 %copy-start.35 = (f32[2,3]{1,0:T(2,128)S(1)}, f32[2,3]{1,0:T(2,128)}, u32[]{:S(2)}) copy-start(f32[2,3]{1,0:T(2,128)} %param.16) | copy-start | bytes 76
  32.7 9.0 %copy-start.31 = (bf16[6,16,16,128]{3,2,1,0:T(8,128)(2,1)S(1)}, bf16[6,16,16,128]{3,2,1,0:T(8,128)(2,1)}, u32[]{:S(2)}) copy-start(bf16[6,16,16,128]{3,2,1,0:T(8,128)(2,1)} %param.9) | copy-start | bytes 1179652
  32.8 11.9 %collective-permute-start.2 = (f32[6,18,1,128]{3,2,1,0:T(1,128)S(1)}, f32[6,18,1,128]{3,2,1,0:T(1,128)}, u32[]{:S(2)}, u32[]{:S(2)}) collective-permute-start(f32[6,18,1,128]{3,2,1,0:T(1,128)S(1)} %get-tuple-element.35), channel_id=1, source_target_pairs={{2,0},{3,1},{6,4},{7,5},{10,8},{11,9},{14,12},{15,13},{18,16},{19,... | collective-permute-start | bytes 165896 | tf_op jit(solution)/shard_map/ppermute | solution.py:18
  34.1 10.6 %collective-permute-start.3 = (f32[6,18,1,128]{3,2,1,0:T(1,128)S(1)}, f32[6,18,1,128]{3,2,1,0:T(1,128)}, u32[]{:S(2)}, u32[]{:S(2)}) collective-permute-start(f32[6,18,1,128]{3,2,1,0:T(1,128)S(1)} %get-tuple-element.34), channel_id=1, source_target_pairs={{0,2},{1,3},{4,6},{5,7},{8,10},{9,11},{12,14},{13,15},{16,18},{17,... | collective-permute-start | bytes 165896 | tf_op jit(solution)/shard_map/ppermute | solution.py:17
  47.8 8.5 %collective-permute-start.4 = (f32[6,18,18,1]{2,1,3,0:T(8,128)}, f32[6,18,18,1]{2,1,3,0:T(8,128)S(1)}, u32[]{:S(2)}, u32[]{:S(2)}) collective-permute-start(f32[6,18,18,1]{2,1,3,0:T(8,128)} %copy.44), channel_id=1, source_target_pairs={{1,0},{3,2},{5,4},{7,6},{9,8},{11,10},{13,12},{15,14},{17,16},{19,... | collective-permute-start | bytes 23336 | tf_op jit(solution)/shard_map/ppermute | solution.py:18
  50.0 7.0 %collective-permute-start.5 = (f32[6,18,18,1]{2,1,3,0:T(8,128)S(1)}, f32[6,18,18,1]{2,1,3,0:T(8,128)}, u32[]{:S(2)}, u32[]{:S(2)}) collective-permute-start(f32[6,18,18,1]{2,1,3,0:T(8,128)S(1)} %copy.46), channel_id=1, source_target_pairs={{0,1},{2,3},{4,5},{6,7},{8,9},{10,11},{12,13},{14,15},{16,17},{18,... | collective-permute-start | bytes 23336 | tf_op jit(solution)/shard_map/ppermute | solution.py:17
  95.3 6.1 %copy-start.2 = (f32[1,16,16,128]{3,2,1,0:T(8,128)}, f32[1,16,16,128]{3,2,1,0:T(8,128)S(1)}, u32[]{:S(2)}) copy-start(f32[1,16,16,128]{3,2,1,0:T(8,128)S(1)} %get-tuple-element.15) | copy-start | bytes 393220
  104.1 13.9 %copy-start.32 = (bf16[6,16,16,128]{3,2,1,0:T(8,128)(2,1)S(1)}, bf16[6,16,16,128]{3,2,1,0:T(8,128)(2,1)}, u32[]{:S(2)}) copy-start(bf16[6,16,16,128]{3,2,1,0:T(8,128)(2,1)} %param.11) | copy-start | bytes 1179652
  104.1 6.1 %collective-permute-start.6 = (f32[6,1,16,128]{3,2,1,0:T(8,128)S(1)}, f32[6,1,16,128]{3,2,1,0:T(8,128)S(1)}, u32[]{:S(2)}, u32[]{:S(2)}) collective-permute-start(f32[6,1,16,128]{3,2,1,0:T(8,128)S(1)} %get-tuple-element.38), channel_id=1, source_target_pairs={{4,0},{8,4},{12,8},{5,1},{9,5},{13,9},{6,2},{10,6},{14,10},{7,3},{... | collective-permute-start | bytes 147464 | tf_op jit(solution)/shard_map/ppermute | solution.py:18
  105.5 6.3 %collective-permute-start.7 = (f32[6,1,16,128]{3,2,1,0:T(8,128)S(1)}, f32[6,1,16,128]{3,2,1,0:T(8,128)S(1)}, u32[]{:S(2)}, u32[]{:S(2)}) collective-permute-start(f32[6,1,16,128]{3,2,1,0:T(8,128)S(1)} %get-tuple-element.37), channel_id=1, source_target_pairs={{0,4},{4,8},{8,12},{1,5},{5,9},{9,13},{2,6},{6,10},{10,14},{3,7},{... | collective-permute-start | bytes 147464 | tf_op jit(solution)/shard_map/ppermute | solution.py:17
  111.9 7.0 %collective-permute-start.8 = (f32[6,18,1,128]{3,2,1,0:T(1,128)S(1)}, f32[6,18,1,128]{3,2,1,0:T(1,128)S(1)}, u32[]{:S(2)}, u32[]{:S(2)}) collective-permute-start(f32[6,18,1,128]{3,2,1,0:T(1,128)S(1)} %get-tuple-element.31), channel_id=1, source_target_pairs={{2,0},{3,1},{6,4},{7,5},{10,8},{11,9},{14,12},{15,13},{18,16},{19,... | collective-permute-start | bytes 165896 | tf_op jit(solution)/shard_map/ppermute | solution.py:18
  113.2 6.3 %collective-permute-start.9 = (f32[6,18,1,128]{3,2,1,0:T(1,128)S(1)}, f32[6,18,1,128]{3,2,1,0:T(1,128)S(1)}, u32[]{:S(2)}, u32[]{:S(2)}) collective-permute-start(f32[6,18,1,128]{3,2,1,0:T(1,128)S(1)} %get-tuple-element.30), channel_id=1, source_target_pairs={{0,2},{1,3},{4,6},{5,7},{8,10},{9,11},{12,14},{13,15},{16,18},{17,... | collective-permute-start | bytes 165896 | tf_op jit(solution)/shard_map/ppermute | solution.py:17
  122.4 6.0 %copy-start.11 = (f32[6,18,1,128]{3,2,1,0:T(1,128)S(1)}, f32[6,18,1,128]{3,2,1,0:T(1,128)}, u32[]{:S(2)}) copy-start(f32[6,18,1,128]{3,2,1,0:T(1,128)} %copy-done.10) | copy-start | bytes 165892
  122.4 6.0 %copy-start.14 = (f32[6,18,1,128]{3,2,1,0:T(1,128)S(1)}, f32[6,18,1,128]{3,2,1,0:T(1,128)}, u32[]{:S(2)}) copy-start(f32[6,18,1,128]{3,2,1,0:T(1,128)} %copy-done.13) | copy-start | bytes 165892
  122.4 7.8 %collective-permute-start.10 = (f32[6,18,18,1]{2,1,3,0:T(8,128)}, f32[6,18,18,1]{2,1,3,0:T(8,128)S(1)}, u32[]{:S(2)}, u32[]{:S(2)}) collective-permute-start(f32[6,18,18,1]{2,1,3,0:T(8,128)} %copy.48), channel_id=1, source_target_pairs={{1,0},{3,2},{5,4},{7,6},{9,8},{11,10},{13,12},{15,14},{17,16},{19,... | collective-permute-start | bytes 23336 | tf_op jit(solution)/shard_map/ppermute | solution.py:18
  124.8 6.2 %collective-permute-start.11 = (f32[6,18,18,1]{2,1,3,0:T(8,128)S(1)}, f32[6,18,18,1]{2,1,3,0:T(8,128)}, u32[]{:S(2)}, u32[]{:S(2)}) collective-permute-start(f32[6,18,18,1]{2,1,3,0:T(8,128)S(1)} %copy.50), channel_id=1, source_target_pairs={{0,1},{2,3},{4,5},{6,7},{8,9},{10,11},{12,13},{14,15},{16,17},{18,... | collective-permute-start | bytes 23336 | tf_op jit(solution)/shard_map/ppermute | solution.py:17
  132.6 3.7 %copy-start.8 = (f32[32768]{0:T(1024)S(1)}, f32[32768]{0:T(1024)}, u32[]{:S(2)}) copy-start(f32[32768]{0:T(1024)} %scatter_custom_fusion) | copy-start | bytes 393220
  132.6 3.7 %copy-start.18 = (f32[6,18,17,128]{3,2,1,0:T(8,128)S(1)}, f32[6,18,17,128]{3,2,1,0:T(8,128)}, u32[]{:S(2)}) copy-start(f32[6,18,17,128]{3,2,1,0:T(8,128)} %get-tuple-element.28) | copy-start | bytes 2820100
  132.6 3.7 %copy-start.19 = (f32[6,18,17,128]{3,2,1,0:T(8,128)S(1)}, f32[6,18,17,128]{3,2,1,0:T(8,128)}, u32[]{:S(2)}) copy-start(f32[6,18,17,128]{3,2,1,0:T(8,128)} %get-tuple-element.29) | copy-start | bytes 2820100
  (24 other events, 44.8 us)
where the time goes:
time: 210 us; the launch traced here: 208 us
  blocking collectives  87.4 us (42%)
  other arithmetic  61.2 us (29%)
  starting transfers between devices  35.9 us (17%)
  local copies, waits for them, and re-layouts  19.4 us (9%)
  waiting for transfers between devices  2.4 us (1%)
    psum x2, blocking collectives, foundation(): total = lax.psum(jnp.sum(mask * field, axis=(1, 2, 3)), ('gx', 'gy', 'col'))  58.9 us
    ppermute x6, starting transfers between devices, with_halo(): before = lax.ppermute(last, axis, up)  27.9 us
    all_gather x1, blocking collectives, shards(): gathered = lax.all_gather(paired[None], ('gx', 'gy'), axis=0, tiled=True)  26 us
    add x12, other arithmetic, navier(): result.append(shear * laplace[channel] + (lame_first + shear) * divergence)  18.1 us
    concatenate x8, other arithmetic, with_halo(): array = jnp.concatenate([before, array, after], axis=dim)  12.4 us
    add x1, other arithmetic, sweep(): diag_real = 8.0 * shear + 2.0 * lame_first - inertia + mask * imp_real  8.89 us
    ppermute x6, starting transfers between devices, with_halo(): after = lax.ppermute(initial, axis, down)  7.99 us
    select_n x2, other arithmetic, material(): lame_first = jnp.where(chosen, table[entry, 0], lame_first)  6.44 us
  transfers between devices with their start and end apart: 12, of which 3 were waited for; matrix products, arithmetic and copies ran while one was open for 18% of the time, Pallas kernels for 0%

commit v1 on v0

--- a/solution.py
+++ b/solution.py
@@ -118,7 +118,9 @@
 
 
 def foundation(field, mask, count):
-    total = lax.psum(jnp.sum(mask * field, axis=(1, 2, 3)), ("gx", "gy", "col"))
+    total = jnp.sum(
+        lax.all_gather(jnp.sum(mask * field, axis=(1, 2, 3)), ("gx", "gy", "col")), axis=0
+    )
     return total / count
 
 

time: 210 us -> 216 us (1.029)
  local copies, waits for them, and re-layouts: 19.4 us -> 21.9 us
  other arithmetic: 61.2 us -> 63.6 us
    unnamed x0 -> x2, blocking collectives: none -> 60 us
    psum x2 -> x0, blocking collectives: 58.9 us -> none  [foundation(): total = lax.psum(jnp.sum(mask * field, axis=(1, 2, 3)), ('gx', 'gy', 'col'))]
  transfers between devices with their start and end apart: 12 -> 12, of which waited for: 3 -> 2; matrix products, arithmetic and copies ran while one was open for 18% -> 17% of each run, Pallas kernels for 0% -> 0%
where the time goes in v1:
time: 216 us; the launch traced here: 215 us
  blocking collectives  88.4 us (41%)
  other arithmetic  63.6 us (29%)
  starting transfers between devices  35.9 us (17%)
  local copies, waits for them, and re-layouts  21.9 us (10%)
  between operations  2.67 us (1%)
  waiting for transfers between devices  2.39 us (1%)
    unnamed x2, blocking collectives  60 us
    ppermute x6, starting transfers between devices, with_halo(): before = lax.ppermute(last, axis, up)  27.9 us
    all_gather x1, blocking collectives, shards(): gathered = lax.all_gather(paired[None], ('gx', 'gy'), axis=0, tiled=True)  26 us
    add x12, other arithmetic, navier(): result.append(shear * laplace[channel] + (lame_first + shear) * divergence)  18.2 us
    concatenate x8, other arithmetic, with_halo(): array = jnp.concatenate([before, array, after], axis=dim)  12.4 us
    add x1, other arithmetic, sweep(): diag_real = 8.0 * shear + 2.0 * lame_first - inertia + mask * imp_real  8.8 us
    ppermute x6, starting transfers between devices, with_halo(): after = lax.ppermute(initial, axis, down)  7.99 us
    select_n x2, other arithmetic, material(): lame_first = jnp.where(chosen, table[entry, 0], lame_first)  6.47 us
  transfers between devices with their start and end apart: 12, of which 2 were waited for; matrix products, arithmetic and copies ran while one was open for 17% of the time, Pallas kernels for 0%

profile of v1, /device:TPU:0, one launch (start us, length us, event | category | flops | bytes accessed | tf_op | source)
XLA Modules:
  0.0 214.9 jit_solution(547567721432669373)
XLA Ops:
  2.7 5.6 %collective-permute-start.1 = (f32[6,1,16,128]{3,2,1,0:T(8,128)S(1)}, f32[6,1,16,128]{3,2,1,0:T(8,128)S(1)}, u32[]{:S(2)}, u32[]{:S(2)}) collective-permute-start(f32[6,1,16,128]{3,2,1,0:T(8,128)S(1)} %get-tuple-element.40), channel_id=1, source_target_pairs={{0,4},{4,8},{8,12},{1,5},{5,9},{9,13},{2,6},{6,10},{10,14},{3,7},{... | collective-permute-start | bytes 147464 | tf_op jit(solution)/shard_map/ppermute | solution.py:17
  8.3 2.0 fusion.108
  11.0 1.9 broadcast_select_fusion
  12.9 4.5 %select_select_fusion.1 = f32[2,8,2,8,4,32]{5,4,3,2,1,0:T(4,128)S(1)} fusion(f32[]{:T(128)} %bitcast, f32[]{:T(128)} %bitcast.1, f32[]{:T(128)} %bitcast.2, f32[]{:T(128)} %bitcast.3, f32[]{:T(128)} %bitcast.4, f32[2,2,4]{2,1,0:T(2,128)S(1)} %get-tuple-element.46, f32[]{:T(128)} %bitcast.6, f32[]{:T(128)} %bitcast.5, ...), kind=kLoop, calls=%fused_computation.41 | loop fusion | flops 229376 | bytes 131276 | tf_op jit(solution)/shard_map/jit(_where)/select_n | solution.py:116
  17.4 4.5 %select_select_fusion = f32[2,8,2,8,4,32]{5,4,3,2,1,0:T(4,128)S(1)} fusion(f32[]{:T(128)} %bitcast.8, f32[]{:T(128)} %bitcast.9, f32[]{:T(128)} %bitcast.10, f32[]{:T(128)} %bitcast.11, f32[]{:T(128)} %bitcast.12, f32[2,2,4]{2,1,0:T(2,128)S(1)} %get-tuple-element.45, f32[]{:T(128)} %bitcast.14, f32[]{:T(128)} %bitcast.13, ...), kind=kLoop, calls=%fused_computation.40 | loop fusion | flops 229376 | bytes 131276 | tf_op jit(solution)/shard_map/jit(_where)/select_n | solution.py:115
  21.9 8.8 %multiply_add_fusion = f32[2,8,2,8,4,32]{5,4,3,2,1,0:T(4,128)S(1)} fusion(f32[2,2,4]{2,1,0:T(2,128)S(1)} %get-tuple-element.46, f32[]{:T(128)} %bitcast.6, pred[2,2,4]{2,1,0:T(4,128)(4,1)S(1)} %get-tuple-element.53, f32[]{:T(128)} %bitcast.5, pred[2,2,4]{2,1,0:T(4,128)(4,1)S(1)} %get-tuple-element.48, f32[]{:T(128)} %bitcast.4, ...), kind=kLoop, calls=%fused_computation.39 | loop fusion | flops 557056 | bytes 131368 | tf_op jit(solution)/shard_map/add | solution.py:94
  34.0 5.8 %collective-permute-start.3 = (f32[6,18,1,128]{3,2,1,0:T(1,128)S(1)}, f32[6,18,1,128]{3,2,1,0:T(1,128)}, u32[]{:S(2)}, u32[]{:S(2)}) collective-permute-start(f32[6,18,1,128]{3,2,1,0:T(1,128)S(1)} %get-tuple-element.34), channel_id=1, source_target_pairs={{0,2},{1,3},{4,6},{5,7},{8,10},{9,11},{12,14},{13,15},{16,18},{17,... | collective-permute-start | bytes 165896 | tf_op jit(solution)/shard_map/ppermute | solution.py:17
  43.8 2.0 scatter_custom_fusion
  51.1 3.7 %collective-permute-start.5 = (f32[6,18,18,1]{2,1,3,0:T(8,128)S(1)}, f32[6,18,18,1]{2,1,3,0:T(8,128)}, u32[]{:S(2)}, u32[]{:S(2)}) collective-permute-start(f32[6,18,18,1]{2,1,3,0:T(8,128)S(1)} %copy.46), channel_id=1, source_target_pairs={{0,1},{2,3},{4,5},{6,7},{8,9},{10,11},{12,13},{14,15},{16,17},{18,... | collective-permute-start | bytes 23336 | tf_op jit(solution)/shard_map/ppermute | solution.py:17
  54.8 2.5 %pad_maximum_fusion.2 = (f32[6,18,17,128]{3,2,1,0:T(8,128)}, f32[6,18,17,128]{3,2,1,0:T(8,128)}) fusion(f32[6,18,1,128]{3,2,1,0:T(1,128)} %collective-permute-done.2, f32[6,1,16,128]{3,2,1,0:T(8,128)S(1)} %collective-permute-done, f32[6,16,16,128]{3,2,1,0:T(8,128)S(1)} %convert_element_type.12, f32[6,1,16,128]{3,2,1,0:T(8,128)S(1)} %collective-permute-done.1, ...), kind=kLoop, calls=%fused_computation.5 | loop fusion | flops 1410048 | bytes 2875392 | tf_op jit(solution)/shard_map/concatenate | solution.py:19
  59.8 3.1 %pad_maximum_fusion = (f32[6,18,18,129]{3,2,1,0:T(8,128)S(1)}, f32[6,18,18,129]{3,2,1,0:T(8,128)S(1)}) fusion(f32[6,18,18,1]{3,2,1,0:T(8,128)S(1)} %copy.45, f32[6,18,1,128]{3,2,1,0:T(1,128)} %collective-permute-done.2, f32[6,1,16,128]{3,2,1,0:T(8,128)S(1)} %collective-permute-done, f32[6,16,16,128]{3,2,1,0:T(8,128)S(1)} %convert_element_type.12, ...), kind=kLoop, calls=%fused_computation.1 | loop fusion | flops 2507760 | bytes 3017088 | tf_op jit(solution)/shard_map/concatenate | solution.py:19
  62.9 2.3 %add_add_fusion.1 = (f32[6,16,16,128]{3,2,1,0:T(8,128)}, f32[6,16,16,128]{3,2,1,0:T(8,128)}, f32[6,16,16,128]{3,2,1,0:T(8,128)}, f32[6,16,16,128]{3,2,1,0:T(8,128)}, f32[6]{0:T(128)S(1)}) fusion(bf16[6,16,16,128]{3,2,1,0:T(8,128)(2,1)S(1)} %copy-done.28, f32[6,18,17,128]{3,2,1,0:T(8,128)S(1)} %copy-done.17, f32[6,18,17,128]{3,2,1,0:T(8,128)S(1)} %copy-done.16, ...), kind=kLoop, calls=%fused_computation.38 | loop fusion | flops 2949114 | bytes 7700504 | tf_op jit(solution)/shard_map/add | solution.py:43
  65.4 30.0 %all-reduce = f32[96]{0:T(128)} all-reduce(f32[96]{0:T(128)S(1)} %dynamic-update-slice), channel_id=2, replica_groups=mesh['freq'=2,'gx'=4,'gy'=2,'col'=2] {'gx','gy','col'}, use_global_device_ids=true, to_apply=%add | all-reduce | flops 96 | bytes 768
  103.7 1.7 fusion.77
  105.5 1.7 fusion.59
  109.5 4.7 %collective-permute-start.7 = (f32[6,1,16,128]{3,2,1,0:T(8,128)S(1)}, f32[6,1,16,128]{3,2,1,0:T(8,128)S(1)}, u32[]{:S(2)}, u32[]{:S(2)}) collective-permute-start(f32[6,1,16,128]{3,2,1,0:T(8,128)S(1)} %get-tuple-element.37), channel_id=1, source_target_pairs={{0,4},{4,8},{8,12},{1,5},{5,9},{9,13},{2,6},{6,10},{10,14},{3,7},{... | collective-permute-start | bytes 147464 | tf_op jit(solution)/shard_map/ppermute | solution.py:17
  117.2 4.5 %collective-permute-start.9 = (f32[6,18,1,128]{3,2,1,0:T(1,128)S(1)}, f32[6,18,1,128]{3,2,1,0:T(1,128)S(1)}, u32[]{:S(2)}, u32[]{:S(2)}) collective-permute-start(f32[6,18,1,128]{3,2,1,0:T(1,128)S(1)} %get-tuple-element.30), channel_id=1, source_target_pairs={{0,2},{1,3},{4,6},{5,7},{8,10},{9,11},{12,14},{13,15},{16,18},{17,... | collective-permute-start | bytes 165896 | tf_op jit(solution)/shard_map/ppermute | solution.py:17
  128.7 3.7 %collective-permute-start.11 = (f32[6,18,18,1]{2,1,3,0:T(8,128)S(1)}, f32[6,18,18,1]{2,1,3,0:T(8,128)}, u32[]{:S(2)}, u32[]{:S(2)}) collective-permute-start(f32[6,18,18,1]{2,1,3,0:T(8,128)S(1)} %copy.50), channel_id=1, source_target_pairs={{0,1},{2,3},{4,5},{6,7},{8,9},{10,11},{12,13},{14,15},{16,17},{18,... | collective-permute-start | bytes 23336 | tf_op jit(solution)/shard_map/ppermute | solution.py:17
  132.4 1.7 pad_maximum_fusion.4
  136.6 3.6 %pad_maximum_fusion.1 = (f32[6,18,18,129]{3,2,1,0:T(8,128)S(1)}, f32[6,18,18,129]{3,2,1,0:T(8,128)S(1)}) fusion(f32[6,18,18,1]{3,2,1,0:T(8,128)S(1)} %copy.49, f32[6,18,1,128]{3,2,1,0:T(1,128)} %copy-done.10, f32[6,1,16,128]{3,2,1,0:T(8,128)S(1)} %collective-permute-done.6, f32[3,16,16,128]{3,2,1,0:T(8,128)S(1)} %divide_add_fusion.2, ...), kind=kLoop, calls=%fused_computation.3 | loop fusion | flops 3009312 | bytes 3017088 | tf_op jit(solution)/shard_map/concatenate | solution.py:19
  140.2 2.3 %add_add_fusion = (f32[6,16,16,128]{3,2,1,0:T(8,128)}, f32[6,16,16,128]{3,2,1,0:T(8,128)}, f32[6,16,16,128]{3,2,1,0:T(8,128)}, f32[6,16,16,128]{3,2,1,0:T(8,128)}, f32[6]{0:T(128)S(1)}) fusion(f32[3,16,16,128]{3,2,1,0:T(8,128)S(1)} %divide_add_fusion.2, f32[3,16,16,128]{3,2,1,0:T(8,128)S(1)} %get-tuple-element.11, f32[6,18,17,128]{3,2,1,0:T(8,128)S(1)} %copy-done.19, ...), kind=kLoop, calls=%fused_computation.36 | loop fusion | flops 3145722 | bytes 7307288 | tf_op jit(solution)/shard_map/add | solution.py:43
  142.7 30.0 %all-reduce.1 = f32[96]{0:T(128)} all-reduce(f32[96]{0:T(128)S(1)} %dynamic-update-slice.1), channel_id=3, replica_groups=mesh['freq'=2,'gx'=4,'gy'=2,'col'=2] {'gx','gy','col'}, use_global_device_ids=true, to_apply=%add.1 | all-reduce | flops 96 | bytes 768
  184.7 2.4 %psum.7 = f32[1,4,4]{2,1,0:T(4,128)S(1)} all-reduce(f32[1,4,4]{2,1,0:T(4,128)S(1)} %bitcast.40), channel_id=1, replica_groups=mesh['freq'=2,'gx'=4,'gy'=2,'col'=2] {'col'}, use_global_device_ids=true, to_apply=%region_8.9 | all-reduce | flops 16 | bytes 128 | tf_op jit(solution)/shard_map/psum | solution.py:165
  187.1 26.0 %all_gather.19 = f32[8,4,4]{2,1,0:T(4,128)S(1)} all-gather(f32[1,4,4]{2,1,0:T(4,128)S(1)} %psum.7), channel_id=1, replica_groups=mesh['freq'=2,'gx'=4,'gy'=2,'col'=2] {'gx','gy'}, dimensions={0}, use_global_device_ids=true | all-gather | bytes 576 | tf_op jit(solution)/shard_map/all_gather | solution.py:166
  (152 shorter events, 53.0 us)
Async XLA Ops:
  0.6 31.0 %copy-start.33 = (bf16[16,16,128]{2,1,0:T(8,128)(2,1)S(1)}, bf16[16,16,128]{2,1,0:T(8,128)(2,1)}, u32[]{:S(2)}) copy-start(bf16[16,16,128]{2,1,0:T(8,128)(2,1)} %param.12) | copy-start | bytes 196612
  1.4 31.1 %collective-permute-start = (f32[6,1,16,128]{3,2,1,0:T(8,128)S(1)}, f32[6,1,16,128]{3,2,1,0:T(8,128)S(1)}, u32[]{:S(2)}, u32[]{:S(2)}) collective-permute-start(f32[6,1,16,128]{3,2,1,0:T(8,128)S(1)} %get-tuple-element.41), channel_id=1, source_target_pairs={{4,0},{8,4},{12,8},{5,1},{9,5},{13,9},{6,2},{10,6},{14,10},{7,3},{... | collective-permute-start | bytes 147464 | tf_op jit(solution)/shard_map/ppermute | solution.py:18
  2.7 29.8 %collective-permute-start.1 = (f32[6,1,16,128]{3,2,1,0:T(8,128)S(1)}, f32[6,1,16,128]{3,2,1,0:T(8,128)S(1)}, u32[]{:S(2)}, u32[]{:S(2)}) collective-permute-start(f32[6,1,16,128]{3,2,1,0:T(8,128)S(1)} %get-tuple-element.40), channel_id=1, source_target_pairs={{0,4},{4,8},{8,12},{1,5},{5,9},{9,13},{2,6},{6,10},{10,14},{3,7},{... | collective-permute-start | bytes 147464 | tf_op jit(solution)/shard_map/ppermute | solution.py:17
  12.9 19.5 %copy-start.34 = (s32[1,256]{1,0:T(1,128)S(1)}, s32[1,256]{1,0:T(1,128)}, u32[]{:S(2)}) copy-start(s32[1,256]{1,0:T(1,128)} %param.15) | copy-start | bytes 3076
  12.9 19.5 %copy-start.27 = (bf16[6,16,16,128]{3,2,1,0:T(8,128)(2,1)S(1)}, bf16[6,16,16,128]{3,2,1,0:T(8,128)(2,1)}, u32[]{:S(2)}) copy-start(bf16[6,16,16,128]{3,2,1,0:T(8,128)(2,1)} %param.10) | copy-start | bytes 1179652
  31.7 8.1 %copy-start.35 = (f32[2,3]{1,0:T(2,128)S(1)}, f32[2,3]{1,0:T(2,128)}, u32[]{:S(2)}) copy-start(f32[2,3]{1,0:T(2,128)} %param.16) | copy-start | bytes 76
  32.5 9.0 %copy-start.31 = (bf16[6,16,16,128]{3,2,1,0:T(8,128)(2,1)S(1)}, bf16[6,16,16,128]{3,2,1,0:T(8,128)(2,1)}, u32[]{:S(2)}) copy-start(bf16[6,16,16,128]{3,2,1,0:T(8,128)(2,1)} %param.9) | copy-start | bytes 1179652
  32.7 9.9 %copy-start.36 = (u32[32]{0:T(128)S(1)}, u32[32]{0:T(128)}, u32[]{:S(2)}) copy-start(u32[32]{0:T(128)} %constant.50) | copy-start | bytes 388
  32.7 13.2 %collective-permute-start.2 = (f32[6,18,1,128]{3,2,1,0:T(1,128)S(1)}, f32[6,18,1,128]{3,2,1,0:T(1,128)}, u32[]{:S(2)}, u32[]{:S(2)}) collective-permute-start(f32[6,18,1,128]{3,2,1,0:T(1,128)S(1)} %get-tuple-element.35), channel_id=1, source_target_pairs={{2,0},{3,1},{6,4},{7,5},{10,8},{11,9},{14,12},{15,13},{18,16},{19,... | collective-permute-start | bytes 165896 | tf_op jit(solution)/shard_map/ppermute | solution.py:18
  34.0 11.9 %collective-permute-start.3 = (f32[6,18,1,128]{3,2,1,0:T(1,128)S(1)}, f32[6,18,1,128]{3,2,1,0:T(1,128)}, u32[]{:S(2)}, u32[]{:S(2)}) collective-permute-start(f32[6,18,1,128]{3,2,1,0:T(1,128)S(1)} %get-tuple-element.34), channel_id=1, source_target_pairs={{0,2},{1,3},{4,6},{5,7},{8,10},{9,11},{12,14},{13,15},{16,18},{17,... | collective-permute-start | bytes 165896 | tf_op jit(solution)/shard_map/ppermute | solution.py:17
  48.9 8.4 %collective-permute-start.4 = (f32[6,18,18,1]{2,1,3,0:T(8,128)}, f32[6,18,18,1]{2,1,3,0:T(8,128)S(1)}, u32[]{:S(2)}, u32[]{:S(2)}) collective-permute-start(f32[6,18,18,1]{2,1,3,0:T(8,128)} %copy.44), channel_id=1, source_target_pairs={{1,0},{3,2},{5,4},{7,6},{9,8},{11,10},{13,12},{15,14},{17,16},{19,... | collective-permute-start | bytes 23336 | tf_op jit(solution)/shard_map/ppermute | solution.py:18
  51.1 7.0 %collective-permute-start.5 = (f32[6,18,18,1]{2,1,3,0:T(8,128)S(1)}, f32[6,18,18,1]{2,1,3,0:T(8,128)}, u32[]{:S(2)}, u32[]{:S(2)}) collective-permute-start(f32[6,18,18,1]{2,1,3,0:T(8,128)S(1)} %copy.46), channel_id=1, source_target_pairs={{0,1},{2,3},{4,5},{6,7},{8,9},{10,11},{12,13},{14,15},{16,17},{18,... | collective-permute-start | bytes 23336 | tf_op jit(solution)/shard_map/ppermute | solution.py:17
  99.2 6.2 %copy-start.2 = (f32[1,16,16,128]{3,2,1,0:T(8,128)}, f32[1,16,16,128]{3,2,1,0:T(8,128)S(1)}, u32[]{:S(2)}) copy-start(f32[1,16,16,128]{3,2,1,0:T(8,128)S(1)} %get-tuple-element.15) | copy-start | bytes 393220
  108.1 13.7 %copy-start.32 = (bf16[6,16,16,128]{3,2,1,0:T(8,128)(2,1)S(1)}, bf16[6,16,16,128]{3,2,1,0:T(8,128)(2,1)}, u32[]{:S(2)}) copy-start(bf16[6,16,16,128]{3,2,1,0:T(8,128)(2,1)} %param.11) | copy-start | bytes 1179652
  108.1 6.2 %collective-permute-start.6 = (f32[6,1,16,128]{3,2,1,0:T(8,128)S(1)}, f32[6,1,16,128]{3,2,1,0:T(8,128)S(1)}, u32[]{:S(2)}, u32[]{:S(2)}) collective-permute-start(f32[6,1,16,128]{3,2,1,0:T(8,128)S(1)} %get-tuple-element.38), channel_id=1, source_target_pairs={{4,0},{8,4},{12,8},{5,1},{9,5},{13,9},{6,2},{10,6},{14,10},{7,3},{... | collective-permute-start | bytes 147464 | tf_op jit(solution)/shard_map/ppermute | solution.py:18
  109.5 6.3 %collective-permute-start.7 = (f32[6,1,16,128]{3,2,1,0:T(8,128)S(1)}, f32[6,1,16,128]{3,2,1,0:T(8,128)S(1)}, u32[]{:S(2)}, u32[]{:S(2)}) collective-permute-start(f32[6,1,16,128]{3,2,1,0:T(8,128)S(1)} %get-tuple-element.37), channel_id=1, source_target_pairs={{0,4},{4,8},{8,12},{1,5},{5,9},{9,13},{2,6},{6,10},{10,14},{3,7},{... | collective-permute-start | bytes 147464 | tf_op jit(solution)/shard_map/ppermute | solution.py:17
  115.9 6.8 %collective-permute-start.8 = (f32[6,18,1,128]{3,2,1,0:T(1,128)S(1)}, f32[6,18,1,128]{3,2,1,0:T(1,128)S(1)}, u32[]{:S(2)}, u32[]{:S(2)}) collective-permute-start(f32[6,18,1,128]{3,2,1,0:T(1,128)S(1)} %get-tuple-element.31), channel_id=1, source_target_pairs={{2,0},{3,1},{6,4},{7,5},{10,8},{11,9},{14,12},{15,13},{18,16},{19,... | collective-permute-start | bytes 165896 | tf_op jit(solution)/shard_map/ppermute | solution.py:18
  117.2 6.3 %collective-permute-start.9 = (f32[6,18,1,128]{3,2,1,0:T(1,128)S(1)}, f32[6,18,1,128]{3,2,1,0:T(1,128)S(1)}, u32[]{:S(2)}, u32[]{:S(2)}) collective-permute-start(f32[6,18,1,128]{3,2,1,0:T(1,128)S(1)} %get-tuple-element.30), channel_id=1, source_target_pairs={{0,2},{1,3},{4,6},{5,7},{8,10},{9,11},{12,14},{13,15},{16,18},{17,... | collective-permute-start | bytes 165896 | tf_op jit(solution)/shard_map/ppermute | solution.py:17
  126.4 6.0 %copy-start.11 = (f32[6,18,1,128]{3,2,1,0:T(1,128)S(1)}, f32[6,18,1,128]{3,2,1,0:T(1,128)}, u32[]{:S(2)}) copy-start(f32[6,18,1,128]{3,2,1,0:T(1,128)} %copy-done.10) | copy-start | bytes 165892
  126.4 6.0 %copy-start.14 = (f32[6,18,1,128]{3,2,1,0:T(1,128)S(1)}, f32[6,18,1,128]{3,2,1,0:T(1,128)}, u32[]{:S(2)}) copy-start(f32[6,18,1,128]{3,2,1,0:T(1,128)} %copy-done.13) | copy-start | bytes 165892
  126.4 7.8 %collective-permute-start.10 = (f32[6,18,18,1]{2,1,3,0:T(8,128)}, f32[6,18,18,1]{2,1,3,0:T(8,128)S(1)}, u32[]{:S(2)}, u32[]{:S(2)}) collective-permute-start(f32[6,18,18,1]{2,1,3,0:T(8,128)} %copy.48), channel_id=1, source_target_pairs={{1,0},{3,2},{5,4},{7,6},{9,8},{11,10},{13,12},{15,14},{17,16},{19,... | collective-permute-start | bytes 23336 | tf_op jit(solution)/shard_map/ppermute | solution.py:18
  128.7 6.2 %collective-permute-start.11 = (f32[6,18,18,1]{2,1,3,0:T(8,128)S(1)}, f32[6,18,18,1]{2,1,3,0:T(8,128)}, u32[]{:S(2)}, u32[]{:S(2)}) collective-permute-start(f32[6,18,18,1]{2,1,3,0:T(8,128)S(1)} %copy.50), channel_id=1, source_target_pairs={{0,1},{2,3},{4,5},{6,7},{8,9},{10,11},{12,13},{14,15},{16,17},{18,... | collective-permute-start | bytes 23336 | tf_op jit(solution)/shard_map/ppermute | solution.py:17
  136.6 3.7 %copy-start.18 = (f32[6,18,17,128]{3,2,1,0:T(8,128)S(1)}, f32[6,18,17,128]{3,2,1,0:T(8,128)}, u32[]{:S(2)}) copy-start(f32[6,18,17,128]{3,2,1,0:T(8,128)} %get-tuple-element.28) | copy-start | bytes 2820100
  136.6 3.7 %copy-start.19 = (f32[6,18,17,128]{3,2,1,0:T(8,128)S(1)}, f32[6,18,17,128]{3,2,1,0:T(8,128)}, u32[]{:S(2)}) copy-start(f32[6,18,17,128]{3,2,1,0:T(8,128)} %get-tuple-element.29) | copy-start | bytes 2820100
  (25 other events, 48.6 us)
